TPU v7x, 32 devices: a whole 2x2x4 slice. The times are simulated.
32 devices in a mesh: slab: 8 (over y, x, core), view: 4 (over z).
Axes of the slice: x: 2, y: 2, z: 4, core: 2. Of those that a mesh axis runs over, the one named last changes fastest.
Arguments:
- estimate: float32 [4, 1024, 1024], P(None, 'slab'), may hold values from 0.5 to 2
- views: float32 [4, 4, 1024, 1024], P('view', None, 'slab'), may hold values from 0.25 to 4
- psf: float32 [4, 1024, 1024], P('view', 'slab'), as said below
- pattern_mult: int32 [4, 8], P('view'), may hold values from 0 to 63
- pattern_shift: int32 [4, 8], P('view'), may hold values from 0 to 127
- interp: float32 [4, 8, 128], P('view'), may hold values from 0.05 to 0.45
Outputs:
- updated: float32 [4, 1024, 1024], P(None, 'slab')
Inputs may be any that keep to these rules, and one draw needn't show every extreme that they name: `psf`: every entry is positive.
All inputs are finite; a program needn't handle non-finite values.
Results may differ from a plain program's by a relative error of at most 0.0001.
Values sent between devices are 32-bit elements; how exact they have to be, the bound alone decides.
No kernel may reach another device: no remote copies, remote signals or barrier semaphores. Data moves between devices by JAX's collectives and lax.ppermute only.
A program may use at most 128 MiB of HBM per device.

v0:
```python
import math
import jax
import jax.numpy as jnp
from jax import lax
from jax.sharding import PartitionSpec as P

highest = lax.Precision.HIGHEST


def block_matrix(multiplier, shifting, weights):
    positions = jnp.arange(128, dtype=jnp.int32)
    first_col = ((2 * multiplier[:, None] + 1) * positions[None, :] + shifting[:, None]) % 128
    second_col = (first_col + 1) % 128
    columns = positions[None, None, :]
    lower = (columns == first_col[:, :, None]).astype(jnp.float32)
    upper = (columns == second_col[:, :, None]).astype(jnp.float32)
    return (1.0 - weights)[:, :, None] * lower + weights[:, :, None] * upper


def angle_tables(rows, cols, length):
    row_index = lax.iota(jnp.int32, rows)[:, None]
    col_index = lax.iota(jnp.int32, cols)[None, :]
    angles = (row_index * col_index % length).astype(jnp.float32) * (2.0 * math.pi / length)
    return (jnp.cos(angles), jnp.sin(angles))


def contract(form, real_part, imag_part, cosine, sine_table, direction, want_imag):
    real_cos = jnp.einsum(form, real_part, cosine, precision=highest)
    if imag_part is None:
        return (real_cos, direction * jnp.einsum(form, real_part, sine_table, precision=highest))
    imag_sin = jnp.einsum(form, imag_part, sine_table, precision=highest)
    out_real = real_cos - direction * imag_sin
    if not want_imag:
        return (out_real, None)
    real_sin = jnp.einsum(form, real_part, sine_table, precision=highest)
    imag_cos = jnp.einsum(form, imag_part, cosine, precision=highest)
    return (out_real, imag_cos + direction * real_sin)


def complex_times(real_part, imag_part, cosine, sine_table):
    return (
        real_part * cosine - imag_part * sine_table,
        real_part * sine_table + imag_part * cosine,
    )


def factored(real_part, imag_part, axis, direction, forward, want_imag):
    length = real_part.shape[axis]
    second = 128
    first = length // second
    if axis == 2:
        leading, trailing = ("rx", "")
    else:
        leading, trailing = ("r", "z")
    outer = real_part.shape
    shape = outer[:axis] + (first, second) + outer[axis + 1 :]
    real_part = real_part.reshape(shape)
    if imag_part is not None:
        imag_part = imag_part.reshape(shape)
    first_cos, first_sin = angle_tables(first, first, first)
    second_cos, second_sin = angle_tables(second, second, second)
    twist_cos, twist_sin = angle_tables(first, second, length)
    if axis == 1:
        twist_cos = twist_cos[:, :, None]
        twist_sin = twist_sin[:, :, None]
    twist_sin = direction * twist_sin
    if forward:
        real_part, imag_part = contract(
            leading + "ab" + trailing + ",ak->" + leading + "kb" + trailing,
            real_part,
            imag_part,
            first_cos,
            first_sin,
            direction,
            True,
        )
        real_part, imag_part = complex_times(real_part, imag_part, twist_cos, twist_sin)
        real_part, imag_part = contract(
            leading + "kb" + trailing + ",bm->" + leading + "km" + trailing,
            real_part,
            imag_part,
            second_cos,
            second_sin,
            direction,
            want_imag,
        )
    else:
        real_part, imag_part = contract(
            leading + "km" + trailing + ",mb->" + leading + "kb" + trailing,
            real_part,
            imag_part,
            second_cos,
            second_sin,
            direction,
            True,
        )
        real_part, imag_part = complex_times(real_part, imag_part, twist_cos, twist_sin)
        real_part, imag_part = contract(
            leading + "kb" + trailing + ",ka->" + leading + "ab" + trailing,
            real_part,
            imag_part,
            first_cos,
            first_sin,
            direction,
            want_imag,
        )
    real_part = real_part.reshape(outer)
    if imag_part is not None:
        imag_part = imag_part.reshape(outer)
    return (real_part, imag_part)


def to_columns(real_part, imag_part):
    depth_real, depth_imag = factored(real_part, imag_part, 2, -1.0, True, True)
    moved_real, moved_imag = (
        lax.all_to_all(depth_real, "slab", split_axis=2, concat_axis=1, tiled=True),
        lax.all_to_all(depth_imag, "slab", split_axis=2, concat_axis=1, tiled=True),
    )
    return factored(moved_real, moved_imag, 1, -1.0, True, True)


def to_planes(real_part, imag_part):
    width_real, width_imag = factored(real_part, imag_part, 1, 1.0, False, True)
    moved_real, moved_imag = (
        lax.all_to_all(width_real, "slab", split_axis=1, concat_axis=2, tiled=True),
        lax.all_to_all(width_imag, "slab", split_axis=1, concat_axis=2, tiled=True),
    )
    scaling = 1.0 / (width_real.shape[1] * moved_real.shape[2])
    out_real, out_imag = factored(moved_real, moved_imag, 2, 1.0, False, False)
    return (out_real * scaling, None)


def shards(estimate, views, psf, pattern_mult, pattern_shift, interp):
    row_count, slab_width, depth = estimate.shape
    blocks = block_matrix(pattern_mult[0], pattern_shift[0], interp[0])
    block_count = depth // 128
    shaped = estimate.reshape(row_count, slab_width, block_count, 128)
    sampled = jnp.einsum("bij,yxbj->yxbi", blocks, shaped, precision=highest).reshape(
        row_count, slab_width, depth
    )

    def pack(volume):
        return (volume, None)

    packed_real, packed_imag = pack(sampled)
    packed_real = jnp.concatenate([packed_real, psf], 0)
    spectra_real, spectra_imag = to_columns(packed_real, packed_imag)
    transfer_real = spectra_real[-1:]
    transfer_imag = spectra_imag[-1:]
    spectra_real = spectra_real[:-1]
    spectra_imag = spectra_imag[:-1]
    filtered_real = spectra_real * transfer_real - spectra_imag * transfer_imag
    filtered_imag = spectra_real * transfer_imag + spectra_imag * transfer_real
    blurred_real, blurred_imag = to_planes(filtered_real, filtered_imag)
    quotient = views[0] / blurred_real
    packed_real, packed_imag = pack(quotient)
    spectra_real, spectra_imag = to_columns(packed_real, packed_imag)
    filtered_real = spectra_real * transfer_real + spectra_imag * transfer_imag
    filtered_imag = spectra_imag * transfer_real - spectra_real * transfer_imag
    smeared_real, smeared_imag = to_planes(filtered_real, filtered_imag)
    correction = jnp.einsum(
        "bij,yxbi->yxbj",
        blocks,
        smeared_real.reshape(row_count, slab_width, block_count, 128),
        precision=highest,
    ).reshape(row_count, slab_width, depth)
    log_terms = jnp.log(correction)
    view_count = lax.axis_size("view")
    summed = lax.psum(log_terms, "view")
    return estimate * jnp.exp(summed / view_count)


def solution(mesh):
    placed = (
        P(None, "slab", None),
        P("view", None, "slab", None),
        P("view", "slab", None),
        P("view", None),
        P("view", None),
        P("view", None, None),
    )
    return jax.shard_map(
        shards, mesh=mesh, in_specs=placed, out_specs=P(None, "slab", None), check_vma=False
    )
```

profile of v0, /device:TPU:0, one launch (start us, length us, event | category | flops | bytes accessed | tf_op | source)
XLA Modules:
  0.0 555.8 jit_solution(18437681724977504398)
XLA Ops:
  10.0 3.6 fusion.121
  15.3 3.1 copy.145
  20.8 4.7 subtract_bitcast_fusion.2
  25.5 3.0 fusion.16
  28.6 3.2 multiply_add_fusion.1
  31.8 3.8 copy.157
  35.7 5.2 all-to-all-start.1
  40.8 3.0 fusion.18
  43.9 3.2 multiply_subtract_fusion.1
  47.1 3.6 copy.151
  50.7 39.3 %all-to-all-done.1 = f32[5,128,1024]{1,0,2:T(8,128)} async-done(((f32[5,128,1024]{1,0,2:T(8,128)}), f32[5,128,1024]{1,0,2:T(8,128)}, u32[]{:S(2)}, u32[]{:S(2)}) %all-to-all-start.1) | async-done | bytes 2621472 | tf_op jit(solution)/shard_map/all_to_all | solution.py:117
  90.0 4.8 all-to-all-start
  95.0 3.1 copy.268
  98.1 3.8 fusion
  101.9 3.9 fusion.2
  105.8 37.9 %all-to-all-done = f32[5,128,1024]{1,0,2:T(8,128)} async-done(((f32[5,128,1024]{1,0,2:T(8,128)}), f32[5,128,1024]{1,0,2:T(8,128)}, u32[]{:S(2)}, u32[]{:S(2)}) %all-to-all-start) | async-done | bytes 2621472 | tf_op jit(solution)/shard_map/all_to_all | solution.py:116
  143.7 3.1 copy.265
  146.8 4.3 multiply_add_fusion
  151.1 3.4 subtract_bitcast_fusion.1
  154.6 2.9 fusion.10
  157.4 2.9 fusion.8
  160.3 3.0 subtract_bitcast_fusion
  163.4 3.0 add_bitcast_fusion
  173.7 2.9 fusion.39
  176.7 3.3 fusion.77
  180.0 2.9 subtract_bitcast_fusion.6
  185.9 4.4 all-to-all-start.2
  190.3 4.5 fusion.75
  194.8 3.0 add_bitcast_fusion.6
  198.1 2.7 copy.181
  200.9 16.1 %all-to-all-done.2 = f32[4,1024,128]{2,0,1:T(4,128)} async-done(((f32[4,1024,128]{2,0,1:T(4,128)}), f32[4,1024,128]{2,0,1:T(4,128)}, u32[]{:S(2)}, u32[]{:S(2)}) %all-to-all-start.2) | async-done | bytes 2097184 | tf_op jit(solution)/shard_map/all_to_all | solution.py:125
  217.0 4.5 all-to-all-start.3
  225.1 3.4 fusion.171
  228.4 19.5 %all-to-all-done.3 = f32[4,1024,128]{2,0,1:T(4,128)} async-done(((f32[4,1024,128]{2,0,1:T(4,128)}), f32[4,1024,128]{2,0,1:T(4,128)}, u32[]{:S(2)}, u32[]{:S(2)}) %all-to-all-start.3) | async-done | bytes 2097184 | tf_op jit(solution)/shard_map/all_to_all | solution.py:126
  256.5 3.1 fusion.47
  259.6 3.3 bitcast_divide_fusion
  269.6 3.0 multiply_add_fusion.5
  275.3 4.4 all-to-all-start.5
  279.6 4.0 fusion.69
  286.3 2.7 copy.189
  289.0 17.3 %all-to-all-done.5 = f32[4,128,1024]{1,0,2:T(4,128)} async-done(((f32[4,128,1024]{1,0,2:T(4,128)}), f32[4,128,1024]{1,0,2:T(4,128)}, u32[]{:S(2)}, u32[]{:S(2)}) %all-to-all-start.5) | async-done | bytes 2097184 | tf_op jit(solution)/shard_map/all_to_all | solution.py:117
  306.3 4.5 all-to-all-start.4
  313.1 3.2 fusion.31
  316.3 3.2 fusion.33
  319.5 17.8 %all-to-all-done.4 = f32[4,128,1024]{1,0,2:T(4,128)} async-done(((f32[4,128,1024]{1,0,2:T(4,128)}), f32[4,128,1024]{1,0,2:T(4,128)}, u32[]{:S(2)}, u32[]{:S(2)}) %all-to-all-start.4) | async-done | bytes 2097184 | tf_op jit(solution)/shard_map/all_to_all | solution.py:116
  339.6 3.7 multiply_add_fusion.4
  360.5 2.8 convolution_subtract_fusion.1
  363.3 2.9 fusion.27
  366.2 2.9 fusion.53
  369.1 2.9 subtract_bitcast_fusion.3
  372.4 2.8 copy.214
  375.3 4.4 all-to-all-start.6
  379.6 4.5 fusion.51
  384.1 3.0 add_bitcast_fusion.3
  387.5 2.7 copy.219
  390.2 16.1 %all-to-all-done.6 = f32[4,1024,128]{2,0,1:T(4,128)} async-done(((f32[4,1024,128]{2,0,1:T(4,128)}), f32[4,1024,128]{2,0,1:T(4,128)}, u32[]{:S(2)}, u32[]{:S(2)}) %all-to-all-start.6) | async-done | bytes 2097184 | tf_op jit(solution)/shard_map/all_to_all | solution.py:125
  406.3 4.3 all-to-all-start.7
  412.6 3.4 fusion.167
  416.0 21.3 %all-to-all-done.7 = f32[4,1024,128]{2,0,1:T(4,128)} async-done(((f32[4,1024,128]{2,0,1:T(4,128)}), f32[4,1024,128]{2,0,1:T(4,128)}, u32[]{:S(2)}, u32[]{:S(2)}) %all-to-all-start.7) | async-done | bytes 2097184 | tf_op jit(solution)/shard_map/all_to_all | solution.py:126
  445.8 2.9 fusion.43
  448.7 3.3 multiply_bitcast_fusion
  457.7 84.9 %all-reduce.2.cloned.1.call-done = f32[4,128,1024]{1,2,0:T(8,128)} async-done(((f32[4,128,1024]{1,2,0:T(8,128)}), f32[4,128,1024]{1,2,0:T(8,128)}) %all-reduce.2.cloned.1.call-update) | async-done | bytes 2097168 | tf_op jit(solution)/shard_map/psum | solution.py:169
  542.6 3.2 exponential_multiply_fusion
  545.8 2.9 copy.226
  (76 shorter events, 81.1 us)
Async XLA Ops:
  18.4 2.4 copy-start
  25.5 3.1 copy-start.1
  35.7 54.4 %all-to-all-start.1 = ((f32[5,128,1024]{1,0,2:T(8,128)}), f32[5,128,1024]{1,0,2:T(8,128)}, u32[]{:S(2)}, u32[]{:S(2)}) async-start(f32[5,128,1024]{1,0,2:T(8,128)} %copy.157), calls=%async_computation.1 | async-start | bytes 8388608 | tf_op jit(solution)/shard_map/all_to_all | solution.py:117
  40.8 3.0 copy-start.2
  90.0 53.7 %all-to-all-start = ((f32[5,128,1024]{1,0,2:T(8,128)}), f32[5,128,1024]{1,0,2:T(8,128)}, u32[]{:S(2)}, u32[]{:S(2)}) async-start(f32[5,128,1024]{1,0,2:T(8,128)} %copy.151), calls=%async_computation | async-start | bytes 8388608 | tf_op jit(solution)/shard_map/all_to_all | solution.py:116
  146.8 4.3 copy-start.6
  176.7 3.3 copy-start.4
  185.9 31.0 %all-to-all-start.2 = ((f32[4,1024,128]{2,0,1:T(4,128)}), f32[4,1024,128]{2,0,1:T(4,128)}, u32[]{:S(2)}, u32[]{:S(2)}) async-start(f32[4,1024,128]{2,0,1:T(4,128)} %copy.176), calls=%async_computation.2 | async-start | bytes 4194304 | tf_op jit(solution)/shard_map/all_to_all | solution.py:125
  200.9 20.6 %copy-start.10 = (f32[1,4,128,1024]{3,2,1,0:T(8,128)S(1)}, f32[1,4,128,1024]{3,2,1,0:T(8,128)}, u32[]{:S(2)}) copy-start(f32[1,4,128,1024]{3,2,1,0:T(8,128)} %param.7) | copy-start | bytes 6291460
  217.0 31.0 %all-to-all-start.3 = ((f32[4,1024,128]{2,0,1:T(4,128)}), f32[4,1024,128]{2,0,1:T(4,128)}, u32[]{:S(2)}, u32[]{:S(2)}) async-start(f32[4,1024,128]{2,0,1:T(4,128)} %copy.181), calls=%async_computation.3 | async-start | bytes 4194304 | tf_op jit(solution)/shard_map/all_to_all | solution.py:126
  249.7 2.1 copy-start.7
  256.5 3.1 copy-start.11
  267.1 2.5 copy-start.5
  275.3 31.0 %all-to-all-start.5 = ((f32[4,128,1024]{1,0,2:T(4,128)}), f32[4,128,1024]{1,0,2:T(4,128)}, u32[]{:S(2)}, u32[]{:S(2)}) async-start(f32[4,128,1024]{1,0,2:T(4,128)} %copy.195), calls=%async_computation.5 | async-start | bytes 4194304 | tf_op jit(solution)/shard_map/all_to_all | solution.py:117
  306.3 31.0 %all-to-all-start.4 = ((f32[4,128,1024]{1,0,2:T(4,128)}), f32[4,128,1024]{1,0,2:T(4,128)}, u32[]{:S(2)}, u32[]{:S(2)}) async-start(f32[4,128,1024]{1,0,2:T(4,128)} %copy.189), calls=%async_computation.4 | async-start | bytes 4194304 | tf_op jit(solution)/shard_map/all_to_all | solution.py:116
  339.6 3.7 copy-start.9
  366.2 2.9 copy-start.3
  375.3 31.0 %all-to-all-start.6 = ((f32[4,1024,128]{2,0,1:T(4,128)}), f32[4,1024,128]{2,0,1:T(4,128)}, u32[]{:S(2)}, u32[]{:S(2)}) async-start(f32[4,1024,128]{2,0,1:T(4,128)} %copy.214), calls=%async_computation.6 | async-start | bytes 4194304 | tf_op jit(solution)/shard_map/all_to_all | solution.py:125
  406.3 31.0 %all-to-all-start.7 = ((f32[4,1024,128]{2,0,1:T(4,128)}), f32[4,1024,128]{2,0,1:T(4,128)}, u32[]{:S(2)}, u32[]{:S(2)}) async-start(f32[4,1024,128]{2,0,1:T(4,128)} %copy.219), calls=%async_computation.7 | async-start | bytes 4194304 | tf_op jit(solution)/shard_map/all_to_all | solution.py:126
  410.6 132.0 %all-reduce.2.cloned.1.call-start = ((), (), s32[]{:S(2)}) async-start(), calls=%async_computation.8 | async-start | bytes 4194304 | tf_op jit(solution)/shard_map/psum | solution.py:169
  439.0 2.1 copy-start.8
  448.7 3.3 copy-start.12
Sparse Core Ops, SparseCore 0:
  455.9 86.6 all-reduce.1
where the time goes:
time: 560 us; the launch traced here: 556 us
  waiting for transfers between devices  270 us (48%)
  matrix products  172 us (31%)
  local copies, waits for them, and re-layouts  55.7 us (10%)
  starting transfers between devices  36.6 us (7%)
  between operations  14.4 us (3%)
  other arithmetic  7.07 us (1%)
    psum x1, waiting for transfers between devices, shards(): summed = lax.psum(log_terms, 'view')  84.9 us
    all_to_all x2, waiting for transfers between devices, to_columns(): lax.all_to_all(depth_imag, 'slab', split_axis=2, concat_axis=1, tiled=True)  56.6 us
    all_to_all x2, waiting for transfers between devices, to_columns(): lax.all_to_all(depth_real, 'slab', split_axis=2, concat_axis=1, tiled=True)  55.7 us
    dot_general x16, matrix products, contract(): real_cos = jnp.einsum(form, real_part, cosine, precision=highest)  48.2 us
    dot_general x14, matrix products, contract(): imag_sin = jnp.einsum(form, imag_part, sine_table, precision=highest)  41.1 us
    all_to_all x2, waiting for transfers between devices, to_planes(): lax.all_to_all(width_imag, 'slab', split_axis=1, concat_axis=2, tiled=True)  40.8 us
    dot_general x12, matrix products, contract(): real_sin = jnp.einsum(form, real_part, sine_table, precision=highest)  36.4 us
    dot_general x12, matrix products, contract(): imag_cos = jnp.einsum(form, imag_part, cosine, precision=highest)  35.7 us
  transfers between devices with their start and end apart: 9, of which 9 were waited for; matrix products, arithmetic and copies ran while one was open for 13% of the time, Pallas kernels for 0%

commit v1 on v0

--- a/solution.py
+++ b/solution.py
@@ -3,8 +3,19 @@
 import jax.numpy as jnp
 from jax import lax
 from jax.sharding import PartitionSpec as P
+from jax.lax import all_to_all, axis_size
 
 highest = lax.Precision.HIGHEST
+
+
+def group_strings(page, device_axis):
+    val = jnp.concatenate(
+        all_to_all(
+            jnp.stack(jnp.split(page, axis_size(device_axis), axis=1), axis=0), device_axis, 0, 0
+        ),
+        axis=2,
+    )
+    return val
 
 
 def block_matrix(multiplier, shifting, weights):
@@ -122,7 +133,7 @@
 def to_planes(real_part, imag_part):
     width_real, width_imag = factored(real_part, imag_part, 1, 1.0, False, True)
     moved_real, moved_imag = (
-        lax.all_to_all(width_real, "slab", split_axis=1, concat_axis=2, tiled=True),
+        group_strings(width_real, "slab"),
         lax.all_to_all(width_imag, "slab", split_axis=1, concat_axis=2, tiled=True),
     )
     scaling = 1.0 / (width_real.shape[1] * moved_real.shape[2])

time: 560 us -> 566 us (1.011)
    unnamed x29 -> x37, local copies, waits for them, and re-layouts: 5.07 us -> 16.6 us
    reshape x4 -> x2, local copies, waits for them, and re-layouts: 11.8 us -> 6.32 us  [factored(): real_part = real_part.reshape(outer)]
where the time goes in v1:
time: 566 us; the launch traced here: 562 us
  waiting for transfers between devices  271 us (48%)
  matrix products  174 us (31%)
  local copies, waits for them, and re-layouts  59.6 us (11%)
  starting transfers between devices  35.1 us (6%)
  between operations  14.4 us (3%)
  other arithmetic  7.08 us (1%)
    psum x1, waiting for transfers between devices, shards(): summed = lax.psum(log_terms, 'view')  84.9 us
    all_to_all x2, waiting for transfers between devices, to_columns(): lax.all_to_all(depth_imag, 'slab', split_axis=2, concat_axis=1, tiled=True)  56.6 us
    all_to_all x2, waiting for transfers between devices, to_columns(): lax.all_to_all(depth_real, 'slab', split_axis=2, concat_axis=1, tiled=True)  55.7 us
    dot_general x16, matrix products, contract(): real_cos = jnp.einsum(form, real_part, cosine, precision=highest)  49.4 us
    dot_general x14, matrix products, contract(): imag_sin = jnp.einsum(form, imag_part, sine_table, precision=highest)  43.5 us
    all_to_all x2, waiting for transfers between devices, to_planes(): lax.all_to_all(width_imag, 'slab', split_axis=1, concat_axis=2, tiled=True)  41.8 us
    dot_general x12, matrix products, contract(): real_sin = jnp.einsum(form, real_part, sine_table, precision=highest)  36.3 us
    dot_general x12, matrix products, contract(): imag_cos = jnp.einsum(form, imag_part, cosine, precision=highest)  35.1 us
  transfers between devices with their start and end apart: 9, of which 9 were waited for; matrix products, arithmetic and copies ran while one was open for 13% of the time, Pallas kernels for 0%

profile of v1, /device:TPU:0, one launch (start us, length us, event | category | flops | bytes accessed | tf_op | source)
XLA Modules:
  0.0 562.1 jit_solution(16927393408936299826)
XLA Ops:
  10.0 3.6 fusion.145
  15.3 3.1 copy.159
  20.8 4.7 subtract_bitcast_fusion.2
  25.6 3.0 fusion.16
  28.6 3.2 multiply_add_fusion.1
  31.9 3.8 copy.171
  35.7 5.2 all-to-all-start.1
  40.8 3.0 fusion.18
  43.9 3.2 multiply_subtract_fusion.1
  47.1 3.6 copy.165
  50.7 39.3 %all-to-all-done.1 = f32[5,128,1024]{1,0,2:T(8,128)} async-done(((f32[5,128,1024]{1,0,2:T(8,128)}), f32[5,128,1024]{1,0,2:T(8,128)}, u32[]{:S(2)}, u32[]{:S(2)}) %all-to-all-start.1) | async-done | bytes 2621472 | tf_op jit(solution)/shard_map/all_to_all | solution.py:128
  90.1 4.8 all-to-all-start
  95.0 3.1 copy.280
  98.1 3.8 fusion
  102.0 3.9 fusion.2
  105.8 37.9 %all-to-all-done = f32[5,128,1024]{1,0,2:T(8,128)} async-done(((f32[5,128,1024]{1,0,2:T(8,128)}), f32[5,128,1024]{1,0,2:T(8,128)}, u32[]{:S(2)}, u32[]{:S(2)}) %all-to-all-start) | async-done | bytes 2621472 | tf_op jit(solution)/shard_map/all_to_all | solution.py:127
  143.8 3.1 copy.277
  146.8 4.3 multiply_add_fusion
  151.2 3.4 subtract_bitcast_fusion.1
  154.6 2.9 fusion.10
  157.5 2.9 fusion.8
  160.3 3.0 subtract_bitcast_fusion
  163.4 3.0 add_bitcast_fusion
  173.8 2.9 fusion.47
  176.7 3.3 fusion.89
  180.0 2.9 fusion.87
  182.9 2.9 subtract_bitcast_fusion.6
  186.1 2.9 add_bitcast_fusion.6
  192.1 4.3 all-to-all-start.3
  202.2 20.9 %all-to-all-done.3 = f32[4,1024,128]{2,0,1:T(4,128)} async-done(((f32[4,1024,128]{2,0,1:T(4,128)}), f32[4,1024,128]{2,0,1:T(4,128)}, u32[]{:S(2)}, u32[]{:S(2)}) %all-to-all-start.3) | async-done | bytes 2097184 | tf_op jit(solution)/shard_map/all_to_all | solution.py:137
  223.1 3.8 all-to-all-start.2
  226.9 3.4 copy.300
  232.0 3.4 fusion.195
  235.4 3.4 fusion.210
  238.8 14.5 %all-to-all-done.2 = f32[8,4,128,128]{3,2,1,0:T(8,128)S(1)} async-done(((f32[8,4,128,128]{3,2,1,0:T(8,128)}), f32[8,4,128,128]{3,2,1,0:T(8,128)S(1)}, u32[]{:S(2)}, u32[]{:S(2)}) %all-to-all-start.2) | async-done | bytes 2097184 | tf_op jit(solution)/shard_map/all_to_all | solution.py:13
  253.3 3.9 fusion.133
  259.7 3.1 fusion.55
  262.8 3.3 bitcast_divide_fusion
  272.8 3.0 multiply_add_fusion.5
  278.5 4.4 all-to-all-start.5
  282.9 4.0 fusion.79
  292.3 17.3 %all-to-all-done.5 = f32[4,128,1024]{1,0,2:T(4,128)} async-done(((f32[4,128,1024]{1,0,2:T(4,128)}), f32[4,128,1024]{1,0,2:T(4,128)}, u32[]{:S(2)}, u32[]{:S(2)}) %all-to-all-start.5) | async-done | bytes 2097184 | tf_op jit(solution)/shard_map/all_to_all | solution.py:128
  309.5 4.5 all-to-all-start.4
  316.3 3.2 fusion.35
  319.5 3.2 fusion.37
  322.7 17.8 %all-to-all-done.4 = f32[4,128,1024]{1,0,2:T(4,128)} async-done(((f32[4,128,1024]{1,0,2:T(4,128)}), f32[4,128,1024]{1,0,2:T(4,128)}, u32[]{:S(2)}, u32[]{:S(2)}) %all-to-all-start.4) | async-done | bytes 2097184 | tf_op jit(solution)/shard_map/all_to_all | solution.py:127
  342.8 3.7 multiply_add_fusion.4
  366.5 2.9 fusion.31
  369.4 2.9 fusion.63
  372.3 2.9 fusion.61
  375.1 3.0 subtract_bitcast_fusion.3
  378.5 2.9 add_bitcast_fusion.3
  384.5 4.3 all-to-all-start.7
  394.6 20.9 %all-to-all-done.7 = f32[4,1024,128]{2,0,1:T(4,128)} async-done(((f32[4,1024,128]{2,0,1:T(4,128)}), f32[4,1024,128]{2,0,1:T(4,128)}, u32[]{:S(2)}, u32[]{:S(2)}) %all-to-all-start.7) | async-done | bytes 2097184 | tf_op jit(solution)/shard_map/all_to_all | solution.py:137
  415.5 3.6 all-to-all-start.6
  421.1 3.4 fusion.192
  424.5 3.4 fusion.207
  427.9 17.8 %all-to-all-done.6 = f32[8,4,128,128]{3,2,1,0:T(8,128)S(1)} async-done(((f32[8,4,128,128]{3,2,1,0:T(8,128)}), f32[8,4,128,128]{3,2,1,0:T(8,128)S(1)}, u32[]{:S(2)}, u32[]{:S(2)}) %all-to-all-start.6) | async-done | bytes 2097184 | tf_op jit(solution)/shard_map/all_to_all | solution.py:13
  445.7 3.9 fusion.139
  452.1 2.9 fusion.51
  455.0 3.3 multiply_bitcast_fusion
  464.0 84.9 %all-reduce.2.cloned.1.call-done = f32[4,128,1024]{1,2,0:T(8,128)} async-done(((f32[4,128,1024]{1,2,0:T(8,128)}), f32[4,128,1024]{1,2,0:T(8,128)}) %all-reduce.2.cloned.1.call-update) | async-done | bytes 2097168 | tf_op jit(solution)/shard_map/psum | solution.py:180
  548.9 3.2 exponential_multiply_fusion
  552.1 2.9 copy.238
  (82 shorter events, 86.9 us)
Async XLA Ops:
  18.4 2.4 copy-start
  25.5 3.1 copy-start.1
  35.7 54.4 %all-to-all-start.1 = ((f32[5,128,1024]{1,0,2:T(8,128)}), f32[5,128,1024]{1,0,2:T(8,128)}, u32[]{:S(2)}, u32[]{:S(2)}) async-start(f32[5,128,1024]{1,0,2:T(8,128)} %copy.171), calls=%async_computation.1 | async-start | bytes 8388608 | tf_op jit(solution)/shard_map/all_to_all | solution.py:128
  40.8 3.1 copy-start.2
  90.1 53.7 %all-to-all-start = ((f32[5,128,1024]{1,0,2:T(8,128)}), f32[5,128,1024]{1,0,2:T(8,128)}, u32[]{:S(2)}, u32[]{:S(2)}) async-start(f32[5,128,1024]{1,0,2:T(8,128)} %copy.165), calls=%async_computation | async-start | bytes 8388608 | tf_op jit(solution)/shard_map/all_to_all | solution.py:127
  146.8 4.3 copy-start.4
  192.1 31.0 %all-to-all-start.3 = ((f32[4,1024,128]{2,0,1:T(4,128)}), f32[4,1024,128]{2,0,1:T(4,128)}, u32[]{:S(2)}, u32[]{:S(2)}) async-start(f32[4,1024,128]{2,0,1:T(4,128)} %copy.194), calls=%async_computation.3 | async-start | bytes 4194304 | tf_op jit(solution)/shard_map/all_to_all | solution.py:137
  223.1 30.2 %all-to-all-start.2 = ((f32[8,4,128,128]{3,2,1,0:T(8,128)}), f32[8,4,128,128]{3,2,1,0:T(8,128)S(1)}, u32[]{:S(2)}, u32[]{:S(2)}) async-start(f32[8,4,128,128]{3,2,1,0:T(8,128)} %fusion.158), calls=%async_computation.2 | async-start | bytes 4194304 | tf_op jit(solution)/shard_map/all_to_all | solution.py:13
  253.3 3.9 copy-start.7
  259.7 3.1 copy-start.8
  270.4 2.5 copy-start.3
  278.5 31.0 %all-to-all-start.5 = ((f32[4,128,1024]{1,0,2:T(4,128)}), f32[4,128,1024]{1,0,2:T(4,128)}, u32[]{:S(2)}, u32[]{:S(2)}) async-start(f32[4,128,1024]{1,0,2:T(4,128)} %copy.208), calls=%async_computation.5 | async-start | bytes 4194304 | tf_op jit(solution)/shard_map/all_to_all | solution.py:128
  309.5 31.0 %all-to-all-start.4 = ((f32[4,128,1024]{1,0,2:T(4,128)}), f32[4,128,1024]{1,0,2:T(4,128)}, u32[]{:S(2)}, u32[]{:S(2)}) async-start(f32[4,128,1024]{1,0,2:T(4,128)} %copy.202), calls=%async_computation.4 | async-start | bytes 4194304 | tf_op jit(solution)/shard_map/all_to_all | solution.py:127
  342.8 3.7 copy-start.5
  384.5 31.0 %all-to-all-start.7 = ((f32[4,1024,128]{2,0,1:T(4,128)}), f32[4,1024,128]{2,0,1:T(4,128)}, u32[]{:S(2)}, u32[]{:S(2)}) async-start(f32[4,1024,128]{2,0,1:T(4,128)} %copy.231), calls=%async_computation.7 | async-start | bytes 4194304 | tf_op jit(solution)/shard_map/all_to_all | solution.py:137
  415.5 30.2 %all-to-all-start.6 = ((f32[8,4,128,128]{3,2,1,0:T(8,128)}), f32[8,4,128,128]{3,2,1,0:T(8,128)S(1)}, u32[]{:S(2)}, u32[]{:S(2)}) async-start(f32[8,4,128,128]{3,2,1,0:T(8,128)} %fusion.150), calls=%async_computation.6 | async-start | bytes 4194304 | tf_op jit(solution)/shard_map/all_to_all | solution.py:13
  419.1 129.8 %all-reduce.2.cloned.1.call-start = ((), (), s32[]{:S(2)}) async-start(), calls=%async_computation.8 | async-start | bytes 4194304 | tf_op jit(solution)/shard_map/psum | solution.py:180
  445.7 3.9 copy-start.6
  455.0 3.3 copy-start.9
Sparse Core Ops, SparseCore 0:
  462.2 86.6 all-reduce.1
